TPU v7x, 32 devices: a whole 2x2x4 slice. The times are simulated.
32 devices in a mesh: section: 2 (over x), dp: 4 (over z), mp: 4 (over y, core).
Axes of the slice: x: 2, y: 2, z: 4, core: 2. Of those that a mesh axis runs over, the one named last changes fastest.
Arguments:
- queries: bfloat16 [2, 4, 640, 4096], P('section', 'dp', None, 'mp')
- keys: bfloat16 [2, 4, 640, 4096], P('section', 'dp', None, 'mp')
- values: bfloat16 [2, 4, 640, 4096], P('section', 'dp', None, 'mp'), may hold values from -6 to 6
- grad_out: bfloat16 [2, 4, 640, 4096], P('section', 'dp', None, 'mp'), may hold values from -6 to 6
- positions: int32 [2, 4, 640], P('section', 'dp'), may hold values from 0 to 319, as said below
Outputs:
- received: bfloat16 [2, 4, 3, 640, 4096], P('section', 'dp', None, 'mp')
- bias_grad: float32 [2, 3, 4096], P('section')
Inputs may be any that keep to these rules, and one draw needn't show every extreme that they name: `positions`: along each sequence a position is 0 or one more than the position before it; the first is 0; a document starts at token 320, and none is longer than 320 tokens.
All inputs are finite; a program needn't handle non-finite values.
Results may differ from a plain program's by a relative error of at most 0.0065.
Values may be sent and summed in bfloat16 or wider, within the bound.
No kernel may reach another device: no remote copies, remote signals or barrier semaphores. Data moves between devices by JAX's collectives and lax.ppermute only.
A program may use at most 64 MiB of HBM per device.

v0:
```python
import math
import jax
import jax.numpy as jnp
from jax import lax
from jax.sharding import PartitionSpec as P

HEAD_DIM = 128


def from_behind(value, axis, steps):
    count = lax.axis_size(axis)
    initial, last = (max(0, -steps), min(count, count - steps))
    return lax.ppermute(value, axis, [(source, source + steps) for source in range(initial, last)])


def per_device(queries, keys, values, grad_out, positions):
    query_rows = queries[0, 0]
    key_rows = keys[0, 0]
    value_rows = values[0, 0]
    grad_rows = grad_out[0, 0]
    token_positions = positions[0, 0]
    length = query_rows.shape[0]
    columns = query_rows.shape[1]
    head_count = columns // HEAD_DIM
    scaling = 1.0 / math.sqrt(HEAD_DIM)
    indices = jnp.arange(length, dtype=jnp.int32)
    allowed = (indices[None, :] <= indices[:, None]) & (
        indices[None, :] >= (indices - token_positions)[:, None]
    )

    def one_head(head, results):
        offset = head * HEAD_DIM
        query_part = lax.dynamic_slice_in_dim(query_rows, offset, HEAD_DIM, 1)
        key_part = lax.dynamic_slice_in_dim(key_rows, offset, HEAD_DIM, 1)
        value_part = lax.dynamic_slice_in_dim(value_rows, offset, HEAD_DIM, 1)
        grad_part = lax.dynamic_slice_in_dim(grad_rows, offset, HEAD_DIM, 1)
        scores = (
            jnp.einsum("qd,kd->qk", query_part, key_part, preferred_element_type=jnp.float32)
            * scaling
        )
        scores = jnp.where(allowed, scores, jnp.float32(-1e30))
        highest = jnp.max(scores, axis=-1, keepdims=True)
        expont = jnp.exp(scores - highest)
        attn = expont / jnp.sum(expont, axis=-1, keepdims=True)
        attn_low = attn.astype(jnp.bfloat16)
        grad_v = jnp.einsum("qk,qd->kd", attn_low, grad_part, preferred_element_type=jnp.float32)
        grad_attn = jnp.einsum(
            "qd,kd->qk", grad_part, value_part, preferred_element_type=jnp.float32
        )
        delta = jnp.sum(attn * grad_attn, axis=-1, keepdims=True)
        grad_scores = (attn * (grad_attn - delta) * scaling).astype(jnp.bfloat16)
        grad_q = jnp.einsum("qk,kd->qd", grad_scores, key_part, preferred_element_type=jnp.float32)
        grad_k = jnp.einsum(
            "qk,qd->kd", grad_scores, query_part, preferred_element_type=jnp.float32
        )
        blocks = jnp.stack([grad_q, grad_k, grad_v]).astype(jnp.bfloat16)
        return lax.dynamic_update_slice_in_dim(results, blocks, offset, 2)

    stacked = lax.fori_loop(0, head_count, one_head, jnp.zeros((3, length, columns), jnp.bfloat16))
    arrived = from_behind(stacked, "section", -1)
    received = lax.all_to_all(arrived, "mp", split_axis=1, concat_axis=2, tiled=True)
    partial_sums = jnp.sum(received.astype(jnp.float32), axis=1)
    totals = lax.psum(partial_sums, ("dp", "mp"))
    bias_grad = totals / math.sqrt(lax.axis_size("dp") * length)
    return (received[None, None], bias_grad[None])


def solution(mesh):
    return jax.shard_map(
        per_device,
        mesh=mesh,
        in_specs=(
            P("section", "dp", None, "mp"),
            P("section", "dp", None, "mp"),
            P("section", "dp", None, "mp"),
            P("section", "dp", None, "mp"),
            P("section", "dp", None),
        ),
        out_specs=(P("section", "dp", None, "mp", None), P("section", None, None)),
        check_vma=False,
    )
```

profile of v0, /device:TPU:0, one launch (start us, length us, event | category | flops | bytes accessed | tf_op | source)
XLA Modules:
  0.0 304.0 jit_solution(6090517974584673321)
XLA Ops:
  1.3 2.4 broadcast_in_dim.30
  3.8 67.3 %while.14 = (s32[]{:T(128)}, bf16[3,640,1024]{2,1,0:T(8,128)(2,1)}, bf16[640,1024]{1,0:T(8,128)(2,1)}, bf16[640,1024]{1,0:T(8,128)(2,1)}, bf16[640,1024]{1,0:T(8...) while((s32[]{:T(128)}, bf16[3,640,1024]{2,1,0:T(8,128)(2,1)}, ...), condition=%wide.region_4.5_spmd.clone, body=%wide.region_0.4_spmd.clone.sunk | while | flops 534608000 | bytes 16580779 | solution.py:59
  3.8 1.4 fusion.43
  6.8 1.5 multiply_reduce_fusion.2
  8.7 1.3 fusion.47
  12.2 1.4 fusion.43
  15.2 1.5 multiply_reduce_fusion.2
  17.1 1.3 fusion.47
  20.6 1.4 fusion.43
  23.6 1.5 multiply_reduce_fusion.2
  25.5 1.3 fusion.47
  29.0 1.4 fusion.43
  32.0 1.5 multiply_reduce_fusion.2
  37.4 1.4 fusion.43
  40.5 1.5 multiply_reduce_fusion.2
  42.4 1.3 fusion.47
  45.8 1.4 fusion.43
  48.9 1.5 multiply_reduce_fusion.2
  50.8 1.3 fusion.47
  54.2 1.4 fusion.43
  57.3 1.5 multiply_reduce_fusion.2
  59.2 1.3 fusion.47
  62.7 1.4 fusion.43
  65.7 1.5 multiply_reduce_fusion.2
  67.6 1.3 fusion.47
  72.4 88.1 %collective-permute-done = bf16[3,640,1024]{2,1,0:T(8,128)(2,1)S(1)} collective-permute-done((bf16[3,640,1024]{2,1,0:T(8,128)(2,1)}, bf16[3,640,1024]{2,1,0:T(8,128)(2,1)S(1)}, u32[]{:S(2)}, u32[]{:S(2)}) %collective-permute-start) | collective-permute-done | bytes 3932192 | tf_op jit(solution)/shard_map/ppermute | solution.py:13
  160.5 3.4 %copy.10 = bf16[3,640,1024]{2,0,1:T(4,128)(2,1)S(1)} copy(bf16[3,640,1024]{2,1,0:T(8,128)(2,1)S(1)} %collective-permute-done) | data formatting | bytes 7864320 | tf_op jit(solution)/shard_map/ppermute | solution.py:13
  163.9 62.8 %all_to_all.15 = bf16[3,640,1024]{2,0,1:T(4,128)(2,1)S(1)} all-to-all(bf16[3,640,1024]{2,0,1:T(4,128)(2,1)S(1)} %copy.10), channel_id=1, replica_groups=mesh['section'=2,'dp'=4,'mp'=4] {'mp'}, dimensions={1} | all-to-all | bytes 7864320 | tf_op jit(solution)/shard_map/all_to_all | solution.py:61
  226.7 2.0 convert_reduce_fusion
  228.7 5.6 %copy.11 = bf16[3,160,4,1024]{3,2,1,0:T(4,128)(2,1)} copy(bf16[3,160,4,1024]{3,0,1,2:T(4,128)(2,1)S(1)} %bitcast.27) | data formatting | bytes 7864320 | tf_op jit(solution)/shard_map/all_to_all | solution.py:61
  234.3 8.6 %broadcast_in_dim.31 = bf16[1,1,3,160,4096]{4,3,2,1,0:T(8,128)(2,1)} reshape(bf16[3,160,4,1024]{3,2,1,0:T(4,128)(2,1)} %copy.11) | data formatting | bytes 7864320 | tf_op jit(solution)/shard_map/broadcast_in_dim | solution.py:65
  242.9 60.4 %psum.7 = f32[3,4096]{1,0:T(4,128)S(1)} all-reduce(f32[3,4096]{1,0:T(4,128)S(1)} %bitcast.30), channel_id=1, replica_groups=mesh['section'=2,'dp'=4,'mp'=4] {'dp','mp'}, use_global_device_ids=true, to_apply=%region_6.7 | all-reduce | flops 12288 | bytes 98304 | tf_op jit(solution)/shard_map/psum | solution.py:63
  (46 shorter events, 37.1 us)
Async XLA Ops:
  71.1 89.4 %collective-permute-start = (bf16[3,640,1024]{2,1,0:T(8,128)(2,1)}, bf16[3,640,1024]{2,1,0:T(8,128)(2,1)S(1)}, u32[]{:S(2)}, u32[]{:S(2)}) collective-permute-start(bf16[3,640,1024]{2,1,0:T(8,128)(2,1)} %get-tuple-element.126), channel_id=1, source_target_pairs={{16,0},{17,1},{18,2},{19,3},{20,4},{21,5},{22,6},{23,7},{24,8},{25... | collective-permute-start | bytes 11796488 | tf_op jit(solution)/shard_map/ppermute | solution.py:13
where the time goes:
time: 305 us; the launch traced here: 304 us
  blocking collectives  123 us (40%)
  waiting for transfers between devices  88.1 us (29%)
  matrix products  54.9 us (18%)
  local copies, waits for them, and re-layouts  20.6 us (7%)
  other arithmetic  14.9 us (5%)
    ppermute x1, waiting for transfers between devices, from_behind(): lax.ppermute(value, axis, [(source, source + steps) for source in range(i...  88.1 us
    all_to_all x1, blocking collectives, per_device(): lax.all_to_all(arrived, 'mp', split_axis=1, concat_axis=2, tiled=True)  62.8 us
    psum x1, blocking collectives, per_device(): totals = lax.psum(partial_sums, ('dp', 'mp'))  60.4 us
    dot_general x8, matrix products, one_head(): jnp.einsum('qd,kd->qk', grad_part, value_part, preferred_element_type=jnp...  11.8 us
    dot_general x8, matrix products, one_head(): jnp.einsum('qd,kd->qk', query_part, key_part, preferred_element_type=jnp....  11.5 us
    dot_general x8, matrix products, one_head(): jnp.einsum('qk,kd->qd', grad_scores, key_part, preferred_element_type=jnp...  10.6 us
    dot_general x8, matrix products, one_head(): jnp.einsum('qk,qd->kd', attn_low, grad_part, preferred_element_type=jnp.f...  10.5 us
    dot_general x8, matrix products, one_head(): jnp.einsum('qk,qd->kd', grad_scores, query_part, preferred_element_type=j...  10.4 us
  transfers between devices with their start and end apart: 1, of which 1 were waited for; matrix products, arithmetic and copies ran while one was open for 0% of the time, Pallas kernels for 0%

commit v1 on v0

--- a/solution.py
+++ b/solution.py
@@ -58,7 +58,10 @@
 
     stacked = lax.fori_loop(0, head_count, one_head, jnp.zeros((3, length, columns), jnp.bfloat16))
     arrived = from_behind(stacked, "section", -1)
-    received = lax.all_to_all(arrived, "mp", split_axis=1, concat_axis=2, tiled=True)
+    received = jnp.concatenate(
+        lax.all_to_all(jnp.stack(jnp.split(arrived, lax.axis_size("mp"), axis=1)), "mp", 0, 0),
+        axis=2,
+    )
     partial_sums = jnp.sum(received.astype(jnp.float32), axis=1)
     totals = lax.psum(partial_sums, ("dp", "mp"))
     bias_grad = totals / math.sqrt(lax.axis_size("dp") * length)

time: 305 us -> 290 us (0.951)
  blocking collectives: 123 us -> 109 us
    all_to_all x1, blocking collectives: 62.8 us -> 48.8 us  [per_device(): lax.all_to_all(jnp.stack(jnp.split(arrived, lax.axis_size('mp'), axis=1))...]
    another operation x0 -> x2, local copies, waits for them, and re-layouts: none -> 9.01 us  [the longest x1 8.6 us: per_device(): return (received[None, None], bias_grad[None])]
    broadcast_in_dim x2 -> x1, local copies, waits for them, and re-layouts: 9.26 us -> 0.65 us  [per_device(): return (received[None, None], bias_grad[None])]
    reshape x0 -> x1, local copies, waits for them, and re-layouts: none -> 7.02 us  [per_device(): jnp.concatenate(lax.all_to_all(jnp.stack(jnp.split(arrived, lax.axis_size...]
    all_to_all x1 -> x0, local copies, waits for them, and re-layouts: 5.59 us -> none  [per_device(): lax.all_to_all(arrived, 'mp', split_axis=1, concat_axis=2, tiled=True)]
    ppermute x1 -> x0, local copies, waits for them, and re-layouts: 3.37 us -> none  [from_behind(): lax.ppermute(value, axis, [(source, source + steps) for source in range(i...]
where the time goes in v1:
time: 290 us; the launch traced here: 289 us
  blocking collectives  109 us (38%)
  waiting for transfers between devices  88.1 us (30%)
  matrix products  54.9 us (19%)
  local copies, waits for them, and re-layouts  20.2 us (7%)
  other arithmetic  14.3 us (5%)
    ppermute x1, waiting for transfers between devices, from_behind(): lax.ppermute(value, axis, [(source, source + steps) for source in range(i...  88.1 us
    psum x1, blocking collectives, per_device(): totals = lax.psum(partial_sums, ('dp', 'mp'))  60.5 us
    all_to_all x1, blocking collectives, per_device(): lax.all_to_all(jnp.stack(jnp.split(arrived, lax.axis_size('mp'), axis=1))...  48.8 us
    dot_general x8, matrix products, one_head(): jnp.einsum('qd,kd->qk', grad_part, value_part, preferred_element_type=jnp...  11.8 us
    dot_general x8, matrix products, one_head(): jnp.einsum('qd,kd->qk', query_part, key_part, preferred_element_type=jnp....  11.5 us
    dot_general x8, matrix products, one_head(): jnp.einsum('qk,kd->qd', grad_scores, key_part, preferred_element_type=jnp...  10.6 us
    dot_general x8, matrix products, one_head(): jnp.einsum('qk,qd->kd', attn_low, grad_part, preferred_element_type=jnp.f...  10.5 us
    dot_general x8, matrix products, one_head(): jnp.einsum('qk,qd->kd', grad_scores, query_part, preferred_element_type=j...  10.4 us
  transfers between devices with their start and end apart: 1, of which 1 were waited for; matrix products, arithmetic and copies ran while one was open for 0% of the time, Pallas kernels for 0%

profile of v1, /device:TPU:0, one launch (start us, length us, event | category | flops | bytes accessed | tf_op | source)
XLA Modules:
  0.0 289.0 jit_solution(3344130509925505434)
XLA Ops:
  1.3 2.4 broadcast_in_dim.27
  3.8 67.3 %while.14 = (s32[]{:T(128)}, bf16[3,640,1024]{2,1,0:T(8,128)(2,1)}, bf16[640,1024]{1,0:T(8,128)(2,1)}, bf16[640,1024]{1,0:T(8,128)(2,1)}, bf16[640,1024]{1,0:T(8...) while((s32[]{:T(128)}, bf16[3,640,1024]{2,1,0:T(8,128)(2,1)}, ...), condition=%wide.region_4.5_spmd.clone, body=%wide.region_0.4_spmd.clone.sunk | while | flops 534608000 | bytes 16580779 | solution.py:59
  3.8 1.4 fusion.43
  6.8 1.5 multiply_reduce_fusion.2
  8.7 1.3 fusion.47
  12.2 1.4 fusion.43
  15.2 1.5 multiply_reduce_fusion.2
  17.1 1.3 fusion.47
  20.6 1.4 fusion.43
  23.6 1.5 multiply_reduce_fusion.2
  25.5 1.3 fusion.47
  29.0 1.4 fusion.43
  32.0 1.5 multiply_reduce_fusion.2
  33.9 1.3 fusion.47
  37.4 1.4 fusion.43
  39.1 1.3 fusion.45
  40.4 1.5 multiply_reduce_fusion.2
  42.4 1.3 fusion.47
  45.8 1.4 fusion.43
  48.9 1.5 multiply_reduce_fusion.2
  50.8 1.3 fusion.47
  54.2 1.4 fusion.43
  57.3 1.5 multiply_reduce_fusion.2
  59.2 1.3 fusion.47
  62.7 1.4 fusion.43
  65.7 1.5 multiply_reduce_fusion.2
  67.6 1.3 fusion.47
  72.4 88.1 %collective-permute-done = bf16[3,640,1024]{2,1,0:T(8,128)(2,1)S(1)} collective-permute-done((bf16[3,640,1024]{2,1,0:T(8,128)(2,1)}, bf16[3,640,1024]{2,1,0:T(8,128)(2,1)S(1)}, u32[]{:S(2)}, u32[]{:S(2)}) %collective-permute-start) | collective-permute-done | bytes 3932192 | tf_op jit(solution)/shard_map/ppermute | solution.py:13
  161.4 48.8 %all_to_all.5 = bf16[4,3,160,1024]{3,2,1,0:T(8,128)(2,1)S(1)} all-to-all(bf16[4,3,160,1024]{3,2,1,0:T(8,128)(2,1)S(1)} %pad_maximum_fusion), channel_id=1, replica_groups=mesh['section'=2,'dp'=4,'mp'=4] {'mp'}, dimensions={0} | all-to-all | bytes 7864320 | tf_op jit(solution)/shard_map/all_to_all | solution.py:62
  212.1 60.5 %psum.7 = f32[3,4096]{1,0:T(4,128)S(1)} all-reduce(f32[3,4096]{1,0:T(4,128)S(1)} %bitcast.36), channel_id=1, replica_groups=mesh['section'=2,'dp'=4,'mp'=4] {'dp','mp'}, use_global_device_ids=true, to_apply=%region_6.7 | all-reduce | flops 12288 | bytes 98304 | tf_op jit(solution)/shard_map/psum | solution.py:66
  273.3 7.0 %copy.8 = bf16[3,160,4,1024]{3,2,1,0:T(4,128)(2,1)} copy(bf16[3,160,4,1024]{3,1,0,2:T(8,128)(2,1)} %bitcast.33) | data formatting | bytes 7864320 | tf_op jit(solution)/shard_map/reshape | solution.py:61
  280.4 8.6 %broadcast_in_dim_reshape.3 = bf16[1,1,3,160,4096]{4,3,2,1,0:T(8,128)(2,1)} reshape(bf16[3,160,4,1024]{3,2,1,0:T(4,128)(2,1)} %copy.8) | data formatting | bytes 7864320 | tf_op jit(solution)/shard_map/broadcast_in_dim;reshape | solution.py:68
  (49 shorter events, 37.3 us)
Async XLA Ops:
  71.1 89.4 %collective-permute-start = (bf16[3,640,1024]{2,1,0:T(8,128)(2,1)}, bf16[3,640,1024]{2,1,0:T(8,128)(2,1)S(1)}, u32[]{:S(2)}, u32[]{:S(2)}) collective-permute-start(bf16[3,640,1024]{2,1,0:T(8,128)(2,1)} %get-tuple-element.126), channel_id=1, source_target_pairs={{16,0},{17,1},{18,2},{19,3},{20,4},{21,5},{22,6},{23,7},{24,8},{25... | collective-permute-start | bytes 11796488 | tf_op jit(solution)/shard_map/ppermute | solution.py:13
  210.2 1.9 copy-start

commit v2 on v0

--- a/solution.py
+++ b/solution.py
@@ -60,7 +60,7 @@
     arrived = from_behind(stacked, "section", -1)
     received = lax.all_to_all(arrived, "mp", split_axis=1, concat_axis=2, tiled=True)
     partial_sums = jnp.sum(received.astype(jnp.float32), axis=1)
-    totals = lax.psum(partial_sums, ("dp", "mp"))
+    totals = jnp.sum(lax.all_gather(partial_sums, ("dp", "mp")), axis=0)
     bias_grad = totals / math.sqrt(lax.axis_size("dp") * length)
     return (received[None, None], bias_grad[None])
 

time: 305 us -> 268 us (0.88)
  blocking collectives: 123 us -> 86.3 us
    psum x1 -> x0, blocking collectives: 60.4 us -> none  [per_device(): totals = lax.psum(partial_sums, ('dp', 'mp'))]
    all_gather x0 -> x1, blocking collectives: none -> 23.5 us  [per_device(): totals = jnp.sum(lax.all_gather(partial_sums, ('dp', 'mp')), axis=0)]
    broadcast_in_dim x2 -> x1, local copies, waits for them, and re-layouts: 9.26 us -> 8.6 us  [per_device(): return (received[None, None], bias_grad[None])]
where the time goes in v2:
time: 268 us; the launch traced here: 267 us
  waiting for transfers between devices  88.1 us (33%)
  blocking collectives  86.3 us (32%)
  matrix products  54.9 us (20%)
  local copies, waits for them, and re-layouts  20.6 us (8%)
  other arithmetic  15 us (6%)
    ppermute x1, waiting for transfers between devices, from_behind(): lax.ppermute(value, axis, [(source, source + steps) for source in range(i...  88.1 us
    all_to_all x1, blocking collectives, per_device(): lax.all_to_all(arrived, 'mp', split_axis=1, concat_axis=2, tiled=True)  62.8 us
    all_gather x1, blocking collectives, per_device(): totals = jnp.sum(lax.all_gather(partial_sums, ('dp', 'mp')), axis=0)  23.5 us
    dot_general x8, matrix products, one_head(): jnp.einsum('qd,kd->qk', grad_part, value_part, preferred_element_type=jnp...  11.8 us
    dot_general x8, matrix products, one_head(): jnp.einsum('qd,kd->qk', query_part, key_part, preferred_element_type=jnp....  11.5 us
    dot_general x8, matrix products, one_head(): jnp.einsum('qk,kd->qd', grad_scores, key_part, preferred_element_type=jnp...  10.6 us
    dot_general x8, matrix products, one_head(): jnp.einsum('qk,qd->kd', attn_low, grad_part, preferred_element_type=jnp.f...  10.5 us
    dot_general x8, matrix products, one_head(): jnp.einsum('qk,qd->kd', grad_scores, query_part, preferred_element_type=j...  10.4 us
  transfers between devices with their start and end apart: 1, of which 1 were waited for; matrix products, arithmetic and copies ran while one was open for 0% of the time, Pallas kernels for 0%

profile of v2, /device:TPU:0, one launch (start us, length us, event | category | flops | bytes accessed | tf_op | source)
XLA Modules:
  0.0 267.3 jit_solution(12472266278593307780)
XLA Ops:
  1.3 2.4 broadcast_in_dim.28
  3.8 67.3 %while.14 = (s32[]{:T(128)}, bf16[3,640,1024]{2,1,0:T(8,128)(2,1)}, bf16[640,1024]{1,0:T(8,128)(2,1)}, bf16[640,1024]{1,0:T(8,128)(2,1)}, bf16[640,1024]{1,0:T(8...) while((s32[]{:T(128)}, bf16[3,640,1024]{2,1,0:T(8,128)(2,1)}, ...), condition=%wide.region_4.5_spmd.clone, body=%wide.region_0.4_spmd.clone.sunk | while | flops 534608000 | bytes 16580779 | solution.py:59
  3.8 1.4 fusion.43
  6.8 1.5 multiply_reduce_fusion.2
  8.7 1.3 fusion.47
  12.2 1.4 fusion.43
  15.2 1.5 multiply_reduce_fusion.2
  17.1 1.3 fusion.47
  20.6 1.4 fusion.43
  23.6 1.5 multiply_reduce_fusion.2
  25.5 1.3 fusion.47
  29.0 1.4 fusion.43
  32.0 1.5 multiply_reduce_fusion.2
  37.4 1.4 fusion.43
  40.5 1.5 multiply_reduce_fusion.2
  42.4 1.3 fusion.47
  45.8 1.4 fusion.43
  48.9 1.5 multiply_reduce_fusion.2
  50.8 1.3 fusion.47
  54.2 1.4 fusion.43
  57.3 1.5 multiply_reduce_fusion.2
  59.2 1.3 fusion.47
  62.7 1.4 fusion.43
  65.7 1.5 multiply_reduce_fusion.2
  67.6 1.3 fusion.47
  72.4 88.1 %collective-permute-done = bf16[3,640,1024]{2,1,0:T(8,128)(2,1)S(1)} collective-permute-done((bf16[3,640,1024]{2,1,0:T(8,128)(2,1)}, bf16[3,640,1024]{2,1,0:T(8,128)(2,1)S(1)}, u32[]{:S(2)}, u32[]{:S(2)}) %collective-permute-start) | collective-permute-done | bytes 3932192 | tf_op jit(solution)/shard_map/ppermute | solution.py:13
  160.5 3.4 %copy.11 = bf16[3,640,1024]{2,0,1:T(4,128)(2,1)S(1)} copy(bf16[3,640,1024]{2,1,0:T(8,128)(2,1)S(1)} %collective-permute-done) | data formatting | bytes 7864320 | tf_op jit(solution)/shard_map/ppermute | solution.py:13
  163.9 62.8 %all_to_all.15 = bf16[3,640,1024]{2,0,1:T(4,128)(2,1)S(1)} all-to-all(bf16[3,640,1024]{2,0,1:T(4,128)(2,1)S(1)} %copy.11), channel_id=1, replica_groups=mesh['section'=2,'dp'=4,'mp'=4] {'mp'}, dimensions={1} | all-to-all | bytes 7864320 | tf_op jit(solution)/shard_map/all_to_all | solution.py:61
  226.7 2.0 convert_reduce_fusion
  228.7 5.6 %copy.12 = bf16[3,160,4,1024]{3,2,1,0:T(4,128)(2,1)} copy(bf16[3,160,4,1024]{3,0,1,2:T(4,128)(2,1)S(1)} %bitcast.27) | data formatting | bytes 7864320 | tf_op jit(solution)/shard_map/all_to_all | solution.py:61
  234.3 8.6 %broadcast_in_dim.29 = bf16[1,1,3,160,4096]{4,3,2,1,0:T(8,128)(2,1)} reshape(bf16[3,160,4,1024]{3,2,1,0:T(4,128)(2,1)} %copy.12) | data formatting | bytes 7864320 | tf_op jit(solution)/shard_map/broadcast_in_dim | solution.py:65
  242.9 23.5 %all_gather.7 = f32[16,3,4096]{2,1,0:T(4,128)S(1)} all-gather(f32[1,3,4096]{2,1,0:T(4,128)S(1)} %bitcast.30), channel_id=1, replica_groups=mesh['section'=2,'dp'=4,'mp'=4] {'dp','mp'}, dimensions={0}, use_global_device_ids=true | all-gather | bytes 835584 | tf_op jit(solution)/shard_map/all_gather | solution.py:63
  (47 shorter events, 37.2 us)
Async XLA Ops:
  71.1 89.4 %collective-permute-start = (bf16[3,640,1024]{2,1,0:T(8,128)(2,1)}, bf16[3,640,1024]{2,1,0:T(8,128)(2,1)S(1)}, u32[]{:S(2)}, u32[]{:S(2)}) collective-permute-start(bf16[3,640,1024]{2,1,0:T(8,128)(2,1)} %get-tuple-element.126), channel_id=1, source_target_pairs={{16,0},{17,1},{18,2},{19,3},{20,4},{21,5},{22,6},{23,7},{24,8},{25... | collective-permute-start | bytes 11796488 | tf_op jit(solution)/shard_map/ppermute | solution.py:13
